TPU v7x, 128 devices: a whole 4x4x4 slice. The times are simulated.
128 devices in a mesh: space: 32 (over x, z, core), feat: 4 (over y).
Axes of the slice: x: 4, y: 4, z: 4, core: 2. Of those that a mesh axis runs over, the one named last changes fastest.
Arguments:
- inputs: bfloat16 [2, 96, 180, 1024], P(None, 'space', None, 'feat'), may hold values from -15 to 15
- cotangent: bfloat16 [2, 96, 180, 1024], P(None, 'space', None, 'feat'), may hold values from -6 to 6
- spec_w1: float32 [2, 8, 128, 128], P(None, 'feat'), may hold values from -0.375 to 0.375
- spec_b1: float32 [2, 1024], P(None, 'feat'), may hold values from -0.3 to 0.3
- spec_w2: float32 [2, 8, 128, 128], P(None, 'feat'), may hold values from -0.375 to 0.375
- spec_b2: float32 [2, 1024], P(None, 'feat'), may hold values from -0.3 to 0.3
- up_weight: bfloat16 [1024, 4096], P(None, 'feat'), may hold values from -0.1875 to 0.1875
- down_weight: bfloat16 [4096, 1024], P('feat'), may hold values from -0.09375 to 0.09375
Outputs:
- output: bfloat16 [2, 96, 180, 1024], P(None, 'space', None, 'feat')
- grad_input: bfloat16 [2, 96, 180, 1024], P(None, 'space', None, 'feat')
All inputs are finite; a program needn't handle non-finite values.
Results may differ from a plain program's by a relative error of at most 0.0102.
Values may be sent and summed in bfloat16 or wider, within the bound.
No kernel may reach another device: no remote copies, remote signals or barrier semaphores. Data moves between devices by JAX's collectives and lax.ppermute only.
A program may use at most 128 MiB of HBM per device.

v0:
```python
import math
import jax
import jax.numpy as jnp
from jax import lax
from jax.sharding import PartitionSpec as P

EPSILON = 1e-05
SHRINK_LEVEL = 0.1
HIGHEST = lax.Precision.HIGHEST


def longitude_tables(width_lon):
    mode_count = width_lon // 2 + 1
    cell_index = jnp.arange(width_lon, dtype=jnp.int32)[:, None]
    wave_number = jnp.arange(mode_count, dtype=jnp.int32)[None, :]
    phase_angle = (
        2.0 * math.pi / width_lon * (cell_index * wave_number % width_lon).astype(jnp.float32)
    )
    scaling = 1.0 / math.sqrt(width_lon)
    cos_fwd = jnp.cos(phase_angle) * scaling
    sin_fwd = -jnp.sin(phase_angle) * scaling
    doubled = jnp.where((wave_number == 0) | (wave_number * 2 == width_lon), 1.0, 2.0).astype(
        jnp.float32
    )
    return (cos_fwd, sin_fwd, cos_fwd * doubled, sin_fwd * doubled)


def padded_tables(width_lon, multiple):
    tables = longitude_tables(width_lon)
    modes = tables[0].shape[1]
    extra = -modes % multiple
    return tuple((jnp.pad(table, ((0, 0), (0, extra))) for table in tables))


def lat_apply(table, field):
    return jnp.einsum("gh,bhkc->bgkc", table, field, precision=HIGHEST)


def complex_latitude(table_cos, table_sin, real_part, imag_part, inverse):
    if inverse:
        return (
            lat_apply(table_cos, real_part) + lat_apply(table_sin, imag_part),
            lat_apply(table_cos, imag_part) - lat_apply(table_sin, real_part),
        )
    return (
        lat_apply(table_cos, real_part) - lat_apply(table_sin, imag_part),
        lat_apply(table_cos, imag_part) + lat_apply(table_sin, real_part),
    )


def lon_forward(field, table):
    return jnp.einsum("brwc,wk->brkc", field, table, precision=HIGHEST)


def lon_back(spec, table):
    return jnp.einsum("brkc,wk->brwc", spec, table, precision=HIGHEST)


def to_blocks(field, block_size):
    return field.reshape(field.shape[:-1] + (field.shape[-1] // block_size, block_size))


def block_mult(field, weights):
    return jnp.einsum("...nc,nce->...ne", field, weights, precision=HIGHEST)


def block_mult_back(field, weights):
    return jnp.einsum("...ne,nce->...nc", field, weights, precision=HIGHEST)


def block_product(real_part, imag_part, weights):
    return (
        block_mult(real_part, weights[0]) - block_mult(imag_part, weights[1]),
        block_mult(real_part, weights[1]) + block_mult(imag_part, weights[0]),
    )


def block_adjoint(real_part, imag_part, weights):
    return (
        block_mult_back(real_part, weights[0]) + block_mult_back(imag_part, weights[1]),
        block_mult_back(imag_part, weights[0]) - block_mult_back(real_part, weights[1]),
    )


def latitude_tables(length):
    index_row = jnp.arange(length, dtype=jnp.int32)
    phase_angle = (
        2.0
        * math.pi
        / length
        * (index_row[:, None] * index_row[None, :] % length).astype(jnp.float32)
    )
    scaling = 1.0 / math.sqrt(length)
    return (jnp.cos(phase_angle) * scaling, -jnp.sin(phase_angle) * scaling)


def to_columns(real_part, imag_part, link_type):
    stacked = jnp.stack([real_part, imag_part]).astype(link_type)
    moved = lax.all_to_all(stacked, "space", 3, 2, tiled=True).astype(jnp.float32)
    return (moved[0], moved[1])


def to_rows(real_part, imag_part, link_type):
    stacked = jnp.stack([real_part, imag_part]).astype(link_type)
    moved = lax.all_to_all(stacked, "space", 2, 3, tiled=True).astype(jnp.float32)
    return (moved[0], moved[1])


def enter_spectrum(real_part, imag_part, tables_lat, link_type=jnp.float32):
    table_cos, table_sin = tables_lat
    real_part, imag_part = to_columns(real_part, imag_part, link_type)
    return complex_latitude(table_cos, table_sin, real_part, imag_part, False)


def leave_spectrum(real_part, imag_part, tables_lat, link_type=jnp.float32):
    table_cos, table_sin = tables_lat
    real_part, imag_part = complex_latitude(table_cos, table_sin, real_part, imag_part, True)
    return to_rows(real_part, imag_part, link_type)


def complex_operator(real_block, imag_block):
    return jnp.stack([jnp.stack([real_block, -imag_block]), jnp.stack([imag_block, real_block])])


def lat_stacked(operator, field, precision=lax.Precision.HIGH):
    return jnp.einsum("pqkh,qbhlc->pbklc", operator, field, precision=precision)


def lon_stacked_forward(field, tables, precision=lax.Precision.HIGH):
    return jnp.einsum("brwc,pwk->pbrkc", field, tables, precision=precision)


def lon_stacked_back(spec, tables, precision=lax.Precision.HIGH):
    return jnp.einsum("pbrkc,pwk->brwc", spec, tables, precision=precision)


def block_operator(weights):
    return jnp.moveaxis(complex_operator(weights[0], weights[1]), 2, 0)


def block_stacked(field, operator):
    return jnp.einsum("qbklnc,npqce->pbklne", field, operator, precision=lax.Precision.HIGH)


def block_stacked_adjoint(field, operator):
    return jnp.einsum("pbklne,npqce->qbklnc", field, operator, precision=lax.Precision.DEFAULT)


def stacked_columns(field, link_type):
    return lax.all_to_all(field.astype(link_type), "space", 3, 2, tiled=True).astype(jnp.float32)


def stacked_rows(field, link_type):
    return lax.all_to_all(field.astype(link_type), "space", 2, 3, tiled=True).astype(jnp.float32)


def token_sums(first_term, second_term):
    pair = jnp.stack([first_term, second_term])
    count = lax.axis_size("feat")
    shifted = jnp.stack(
        [pair]
        + [
            lax.ppermute(pair, "feat", [(i, (i + count - shift) % count) for i in range(count)])
            for shift in range(1, count)
        ]
    )
    total = shifted[0]
    for source in range(1, count):
        total = total + shifted[source]
    return (total[0], total[1])


def ring_send(block):
    count = lax.axis_size("feat")
    return [block] + [
        lax.ppermute(block, "feat", [(i, (i + shift) % count) for i in range(count)])
        for shift in range(1, count)
    ]


def ring_assemble(parts):
    count = len(parts)
    position = lax.axis_index("feat")
    block = parts[0]
    width = block.shape[-1]
    whole = jnp.zeros(block.shape[:-1] + (width * count,), block.dtype)
    for shift, moved in enumerate(parts):
        source = (position + count - shift) % count
        whole = lax.dynamic_update_slice_in_dim(whole, moved, source * width, axis=block.ndim - 1)
    return whole


def channel_share(term):
    return lax.psum_scatter(
        term.astype(jnp.bfloat16), "feat", scatter_dimension=3, tiled=True
    ).astype(jnp.float32)


def gelu_value(field):
    return 0.5 * field * (1.0 + lax.erf(field * (1.0 / math.sqrt(2.0))))


def gelu_slope(field):
    return 0.5 * (1.0 + lax.erf(field * (1.0 / math.sqrt(2.0)))) + field * jnp.exp(
        -0.5 * field * field
    ) * (1.0 / math.sqrt(2.0 * math.pi))


def per_device(inputs, cotangent, spec_w1, spec_b1, spec_w2, spec_b2, up_weight, down_weight):
    full_width = up_weight.shape[0]
    block_size = spec_w1.shape[2]
    tables_lon = padded_tables(inputs.shape[2], lax.axis_size("space"))
    tables_lat = latitude_tables(inputs.shape[1] * lax.axis_size("space"))
    cos_fwd, sin_fwd, cos_inv, sin_inv = tables_lon
    table_cos, table_sin = tables_lat
    operators = (
        jnp.stack([cos_fwd, sin_fwd]),
        jnp.stack([cos_inv, sin_inv]),
        complex_operator(table_cos, table_sin),
        complex_operator(table_cos, -table_sin),
        block_operator(spec_w1),
        block_operator(spec_w2),
    )
    operators = lax.optimization_barrier(operators)
    lon_fwd_tables, lon_inv_tables, lat_forward_op, lat_inverse_op, first_op, second_op = operators
    values = inputs.astype(jnp.float32)
    cotangent_parts = lax.all_gather(cotangent, "feat", axis=3, tiled=True)
    first_sum, second_sum = token_sums(jnp.sum(values, axis=-1), jnp.sum(values * values, axis=-1))
    mean_one = first_sum[..., None] / full_width
    rstd_one = lax.rsqrt(second_sum[..., None] / full_width - mean_one * mean_one + EPSILON)
    normed = (values - mean_one) * rstd_one
    spec = lat_stacked(
        lat_forward_op, stacked_columns(lon_stacked_forward(normed, lon_fwd_tables), jnp.float32)
    )
    spec_blocks = to_blocks(spec, block_size)
    bias_one = to_blocks(spec_b1, block_size)[:, None, None, None]
    bias_two = to_blocks(spec_b2, block_size)[:, None, None, None]
    first = jax.nn.relu(block_stacked(spec_blocks, first_op) + bias_one)
    second = block_stacked(first, second_op) + bias_two
    shrunk = (second - jnp.clip(second, -SHRINK_LEVEL, SHRINK_LEVEL)).reshape(spec.shape)
    shrunk, cotangent_parts = lax.optimization_barrier((shrunk, cotangent_parts))
    whole_cotangent = cotangent_parts
    filtered = lon_stacked_back(
        stacked_rows(lat_stacked(lat_inverse_op, shrunk, lax.Precision.DEFAULT), jnp.bfloat16),
        lon_inv_tables,
        lax.Precision.DEFAULT,
    )
    residual = (filtered + normed + values).astype(jnp.bfloat16)
    residual_vals = residual.astype(jnp.float32)
    whole_residual = lax.all_gather(residual, "feat", axis=3, tiled=True)
    grad_act = jnp.einsum(
        "brwd,hd->brwh", whole_cotangent, down_weight, preferred_element_type=jnp.float32
    )
    whole_residual, grad_act = lax.optimization_barrier((whole_residual, grad_act))
    whole_vals = whole_residual.astype(jnp.float32)
    mean_two = jnp.sum(whole_vals, axis=-1, keepdims=True) / full_width
    square_two = jnp.sum(whole_vals * whole_vals, axis=-1, keepdims=True) / full_width
    rstd_two = lax.rsqrt(square_two - mean_two * mean_two + EPSILON)
    vhat = (whole_vals - mean_two) * rstd_two
    hidden = jnp.einsum(
        "brwd,dh->brwh", vhat.astype(jnp.bfloat16), up_weight, preferred_element_type=jnp.float32
    )
    activated = gelu_value(hidden).astype(jnp.bfloat16)
    mixed_term = jnp.einsum(
        "brwh,hd->brwd", activated, down_weight, preferred_element_type=jnp.float32
    )
    output = (residual_vals + channel_share(mixed_term)).astype(jnp.bfloat16)
    grad_hidden = (grad_act * gelu_slope(hidden)).astype(jnp.bfloat16)
    grad_term = jnp.einsum(
        "brwh,dh->brwd", grad_hidden, up_weight, preferred_element_type=jnp.float32
    )
    total_one, total_two = token_sums(
        jnp.sum(grad_term, axis=-1), jnp.sum(grad_term * vhat, axis=-1)
    )
    grad_vhat = channel_share(grad_term)
    own_hat = (residual_vals - mean_two) * rstd_two
    grad_residual = cotangent.astype(jnp.float32) + rstd_two * (
        grad_vhat
        - total_one[..., None] / full_width
        - own_hat * (total_two[..., None] / full_width)
    )
    grad_spec = lat_stacked(
        lat_forward_op,
        stacked_columns(
            lon_stacked_forward(grad_residual, lon_inv_tables, lax.Precision.DEFAULT), jnp.bfloat16
        ),
        lax.Precision.DEFAULT,
    )
    grad_second = jnp.where(jnp.abs(second) > SHRINK_LEVEL, to_blocks(grad_spec, block_size), 0.0)
    grad_first = jnp.where(first > 0.0, block_stacked_adjoint(grad_second, second_op), 0.0)
    grad_spectrum = block_stacked_adjoint(grad_first, first_op).reshape(spec.shape)
    grad_normed = grad_residual + lon_stacked_back(
        stacked_rows(
            lat_stacked(lat_inverse_op, grad_spectrum, lax.Precision.DEFAULT), jnp.bfloat16
        ),
        lon_fwd_tables,
        lax.Precision.DEFAULT,
    )
    norm_one, norm_two = token_sums(
        jnp.sum(grad_normed, axis=-1), jnp.sum(grad_normed * normed, axis=-1)
    )
    grad_input = grad_residual + rstd_one * (
        grad_normed - norm_one[..., None] / full_width - normed * (norm_two[..., None] / full_width)
    )
    return (output, grad_input.astype(jnp.bfloat16))


def solution(mesh):
    return jax.shard_map(
        per_device,
        mesh=mesh,
        in_specs=(
            P(None, "space", None, "feat"),
            P(None, "space", None, "feat"),
            P(None, "feat", None, None),
            P(None, "feat"),
            P(None, "feat", None, None),
            P(None, "feat"),
            P(None, "feat"),
            P("feat", None),
        ),
        out_specs=(P(None, "space", None, "feat"), P(None, "space", None, "feat")),
        check_vma=False,
    )
```

profile of v0, /device:TPU:1, one launch (start us, length us, event | category | flops | bytes accessed | tf_op | source)
XLA Modules:
  0.0 219.6 jit_solution(13806531281613694137)
XLA Ops:
  7.2 1.7 convert_reduce_fusion.1
  9.0 3.8 %collective-permute-start.1 = (f32[2,2,3,180]{3,2,1,0:T(4,128)S(1)}, f32[2,2,3,180]{3,2,1,0:T(4,128)S(1)}, u32[]{:S(2)}, u32[]{:S(2)}) collective-permute-start(f32[2,2,3,180]{3,2,1,0:T(4,128)S(1)} %pad_maximum_fusion.8), channel_id=1, source_target_pairs={{0,2},{1,3},{2,0},{3,1},{4,6},{5,7},{6,4},{7,5},{8,10},{9,11},{10,... | collective-permute-start | bytes 25928 | tf_op jit(solution)/shard_map/ppermute | solution.py:163
  13.2 2.3 %collective-permute-start = (f32[2,2,3,180]{3,2,1,0:T(4,128)S(1)}, f32[2,2,3,180]{3,2,1,0:T(4,128)S(1)}, u32[]{:S(2)}, u32[]{:S(2)}) collective-permute-start(f32[2,2,3,180]{3,2,1,0:T(4,128)S(1)} %pad_maximum_fusion.8), channel_id=1, source_target_pairs={{0,3},{1,0},{2,1},{3,2},{4,7},{5,4},{6,5},{7,6},{8,11},{9,8},{10,9... | collective-permute-start | bytes 25928 | tf_op jit(solution)/shard_map/ppermute | solution.py:163
  22.0 28.2 %all_to_all.72 = f32[2,2,3,96,256]{4,1,2,0,3:T(2,128)S(1)} all-to-all(f32[2,2,3,96,256]{4,1,2,0,3:T(2,128)S(1)} %copy.96), channel_id=1, replica_groups=mesh['space'=32,'feat'=4] {'space'}, dimensions={3} | all-to-all | bytes 2359296 | tf_op jit(solution)/shard_map/all_to_all | solution.py:150
  51.3 1.6 reshape.195
  52.9 2.1 fusion.31
  59.8 16.0 %all_to_all.73 = bf16[2,2,96,3,256]{4,0,3,1,2:T(2,128)(2,1)S(1)} all-to-all(bf16[2,2,96,3,256]{4,0,3,1,2:T(2,128)(2,1)S(1)} %copy.108), channel_id=1, replica_groups=mesh['space'=32,'feat'=4] {'space'}, dimensions={2} | all-to-all | bytes 1179648 | tf_op jit(solution)/shard_map/all_to_all | solution.py:154
  77.6 6.9 %fusion.16 = f32[2,3,180,1024]{3,2,1,0:T(8,128)} fusion(bf16[2,3,180,1024]{3,0,2,1:T(2,128)(2,1)} %all-gather.3.cloned.1.call-done, bf16[1024,1024]{1,0:T(8,128)(2,1)} %param.15), kind=kOutput, calls=%fused_computation.20 | convolution fusion | flops 2264924160 | bytes 8732672 | tf_op jit(solution)/shard_map/brwd,hd->brwh/dot_general | solution.py:251
  84.5 23.0 %all-gather.5.cloned.1.call-done = bf16[2,3,180,1024]{3,2,1,0:T(8,128)(2,1)} async-done(((bf16[2,3,180,256]{3,2,1,0:T(8,128)(2,1)}), bf16[2,3,180,1024]{3,2,1,0:T(8,128)(2,1)}) %all-gather.5.cloned.1.call-update) | async-done | bytes 2211856 | tf_op jit(solution)/shard_map/all_gather | solution.py:250
  107.6 2.5 %convert_reduce_fusion = (f32[2,3,180]{2,1,0:T(4,128)S(1)}, f32[2,3,180]{2,1,0:T(4,128)S(1)}) fusion(bf16[2,3,180,1024]{3,2,1,0:T(8,128)(2,1)} %all-gather.5.cloned.1.call-done), kind=kLoop, calls=%fused_computation.3 | loop fusion | flops 4421520 | bytes 2220480 | tf_op jit(solution)/shard_map/reduce_sum | solution.py:256
  110.2 2.8 %fusion.14 = f32[2,3,180,1024]{3,2,1,0:T(8,128)S(1)} fusion(bf16[2,3,180,1024]{3,2,1,0:T(8,128)(2,1)S(1)} %copy-done.8, f32[2,3,180]{2,1,0:T(4,128)S(1)} %get-tuple-element.60, f32[2,3,180]{2,1,0:T(4,128)S(1)} %get-tuple-element.59, bf16[1024,1024]{1,0:T(8,128)(2,1)S(1)} %copy-done), kind=kOutput, calls=%fused_computation.19 | convolution fusion | flops 2269347840 | bytes 8741312 | tf_op jit(solution)/shard_map/brwd,dh->brwh/dot_general | solution.py:260
  113.1 5.4 %fusion.123 = (f32[2,3,180]{2,1,0:T(4,128)S(1)}, f32[2,3,180]{2,1,0:T(4,128)S(1)}, bf16[2,3,180,1024]{3,2,1,0:T(8,128)(2,1)}) fusion(f32[2,3,180]{2,1,0:T(4,128)S(1)} %get-tuple-element.60, f32[2,3,180]{2,1,0:T(4,128)S(1)} %get-tuple-element.59, bf16[2,3,180,1024]{3,2,1,0:T(8,128)(2,1)S(1)} %copy-done.8, bf16[1024,1024]{1,0:T(8,128)(2,1)S(1)} %copy-done, ...), kind=kOutput, calls=%fused_computation.189 | convolution fusion | flops 2283722752 | bytes 15385472 | tf_op jit(solution)/shard_map/brwh,dh->brwd/dot_general | solution.py:269
  118.5 6.9 %fusion.28 = bf16[2,3,180,1024]{3,2,1,0:T(8,128)(2,1)} fusion(bf16[1024,1024]{1,0:T(8,128)(2,1)} %param.15, f32[2,3,180,1024]{3,2,1,0:T(8,128)} %copy-done.19), kind=kOutput, calls=%fused_computation.36 | convolution fusion | flops 2271559680 | bytes 8732672 | tf_op jit(solution)/shard_map/brwh,hd->brwd/dot_general | solution.py:264
  125.5 2.5 %collective-permute-start.4 = (f32[2,2,3,180]{3,2,1,0:T(4,128)S(1)}, f32[2,2,3,180]{3,2,1,0:T(4,128)S(1)}, u32[]{:S(2)}, u32[]{:S(2)}) collective-permute-start(f32[2,2,3,180]{3,2,1,0:T(4,128)S(1)} %pad_maximum_fusion.9), channel_id=1, source_target_pairs={{0,2},{1,3},{2,0},{3,1},{4,6},{5,7},{6,4},{7,5},{8,10},{9,11},{10,... | collective-permute-start | bytes 25928 | tf_op jit(solution)/shard_map/ppermute | solution.py:163
  128.0 2.7 %collective-permute-start.3 = (f32[2,2,3,180]{3,2,1,0:T(4,128)S(1)}, f32[2,2,3,180]{3,2,1,0:T(4,128)S(1)}, u32[]{:S(2)}, u32[]{:S(2)}) collective-permute-start(f32[2,2,3,180]{3,2,1,0:T(4,128)S(1)} %pad_maximum_fusion.9), channel_id=1, source_target_pairs={{0,3},{1,0},{2,1},{3,2},{4,7},{5,4},{6,5},{7,6},{8,11},{9,8},{10,9... | collective-permute-start | bytes 25928 | tf_op jit(solution)/shard_map/ppermute | solution.py:163
  132.0 19.8 %reduce-scatter.5.cloned.1.call-done = bf16[2,3,180,256]{3,2,1,0:T(8,128)(2,1)} async-done(((bf16[2,3,180,1024]{3,2,1,0:T(8,128)(2,1)}), bf16[2,3,180,256]{3,2,1,0:T(8,128)(2,1)}) %reduce-scatter.5.cloned.1.call-update) | async-done | bytes 552976 | tf_op jit(solution)/shard_map/reduce_scatter | solution.py:194
  151.8 2.3 %fusion.40 = bf16[2,2,3,96,256]{4,3,2,1,0:T(8,128)(2,1)S(1)} fusion(bf16[2,180,96]{2,1,0:T(8,128)(2,1)} %pad_maximum_fusion.3, bf16[2,3,180,256]{3,2,1,0:T(8,128)(2,1)} %fusion.37, bf16[2,3,180,256]{3,2,1,0:T(8,128)(2,1)} %reduce-scatter.5.cloned.1.call-done, bf16[2,3,180,256]{3,0,2,1:T(2,128)(2,1)} %param.9, f32[2,3,180]{2,1,0:T(4,128)S(1)} %get-tuple-element.58, ...), kind=kOutput, calls=%fused_computation.61 | convolution fusion | flops 108933120 | bytes 2335104 | tf_op jit(solution)/shard_map/brwc,pwk->pbrkc/dot_general | solution.py:130
  154.7 19.7 %all_to_all.74 = bf16[2,2,3,96,256]{4,1,2,0,3:T(2,128)(2,1)S(1)} all-to-all(bf16[2,2,3,96,256]{4,1,2,0,3:T(2,128)(2,1)S(1)} %copy.114), channel_id=1, replica_groups=mesh['space'=32,'feat'=4] {'space'}, dimensions={3} | all-to-all | bytes 1179648 | tf_op jit(solution)/shard_map/all_to_all | solution.py:150
  176.0 2.5 %reshape.229 = bf16[2,2,96,3,2,128]{5,4,2,0,3,1:T(2,128)(2,1)} reshape(bf16[2,2,96,3,256]{4,2,0,3,1:T(8,128)(2,1)} %convolution_bitcast_fusion.8) | data formatting | bytes 1179648 | tf_op jit(solution)/shard_map/reshape | solution.py:60
  178.5 2.1 fusion.39
  183.0 15.9 %all_to_all.75 = bf16[2,2,96,3,256]{4,0,3,1,2:T(2,128)(2,1)S(1)} all-to-all(bf16[2,2,96,3,256]{4,0,3,1,2:T(2,128)(2,1)S(1)} %copy.126), channel_id=1, replica_groups=mesh['space'=32,'feat'=4] {'space'}, dimensions={2} | all-to-all | bytes 1179648 | tf_op jit(solution)/shard_map/all_to_all | solution.py:154
  199.4 2.7 %fusion.124 = (f32[2,3,180]{2,1,0:T(4,128)S(1)}, f32[2,3,180]{2,1,0:T(4,128)S(1)}, f32[2,3,180,256]{3,2,1,0:T(8,128)}) fusion(f32[2,3,180]{2,1,0:T(4,128)S(1)} %fusion.115, f32[2,3,180]{2,1,0:T(4,128)S(1)} %fusion.116, bf16[2,3,180,256]{3,0,2,1:T(2,128)(2,1)S(1)} %copy-done.4, bf16[2,2,3,96,256]{4,1,3,2,0:T(2,128)(2,1)S(1)} %bitcast.284, ...), kind=kOutput, calls=%fused_computation.190 | convolution fusion | flops 110866320 | bytes 4080384 | tf_op jit(solution)/shard_map/pbrkc,pwk->brwc/dot_general | solution.py:134
  203.4 2.6 %collective-permute-start.6 = (f32[2,2,3,180]{3,2,1,0:T(4,128)S(1)}, f32[2,2,3,180]{3,2,1,0:T(4,128)S(1)}, u32[]{:S(2)}, u32[]{:S(2)}) collective-permute-start(f32[2,2,3,180]{3,2,1,0:T(4,128)S(1)} %pad_maximum_fusion.10), channel_id=1, source_target_pairs={{0,3},{1,0},{2,1},{3,2},{4,7},{5,4},{6,5},{7,6},{8,11},{9,8},{10,9... | collective-permute-start | bytes 25928 | tf_op jit(solution)/shard_map/ppermute | solution.py:163
  207.3 3.4 %fusion.68 = (bf16[2,3,180,256]{3,2,1,0:T(8,128)(2,1)S(1)}, bf16[2,3,180,256]{3,2,1,0:T(8,128)(2,1)S(1)}) fusion(f32[2,3,180,256]{3,2,1,0:T(8,128)} %get-tuple-element.64, f32[2,3,180]{2,1,0:T(4,128)S(1)} %get-tuple-element.56, f32[2,3,180]{2,1,0:T(4,128)S(1)} %get-tuple-element.55, f32[2,3,180]{2,1,0:T(4,128)S(1)} %fusion.115, ...), kind=kLoop, calls=%fused_computation.92 | loop fusion | flops 6082560 | bytes 5011200 | tf_op jit(solution)/shard_map/convert_element_type | solution.py:305
  (119 shorter events, 25.8 us)
Async XLA Ops:
  7.2 103.0 %copy-start = (bf16[1024,1024]{1,0:T(8,128)(2,1)S(1)}, bf16[1024,1024]{1,0:T(8,128)(2,1)}, u32[]{:S(2)}) copy-start(bf16[1024,1024]{1,0:T(8,128)(2,1)} %param.14) | copy-start | bytes 6291460
  7.2 10.1 %copy-start.14 = (f32[2,2,128,128]{3,2,1,0:T(8,128)S(1)}, f32[2,2,128,128]{3,2,1,0:T(8,128)}, u32[]{:S(2)}) copy-start(f32[2,2,128,128]{3,2,1,0:T(8,128)} %param.10) | copy-start | bytes 786436
  7.2 50.5 %all-gather.3.cloned.1.call-start = ((), (), s32[]{:S(2)}) async-start(), calls=%async_computation.6 | async-start | bytes 2764800 | tf_op jit(solution)/shard_map/all_gather | solution.py:227
  9.0 8.4 %copy-start.15 = (f32[2,2,128,128]{3,2,1,0:T(8,128)S(1)}, f32[2,2,128,128]{3,2,1,0:T(8,128)}, u32[]{:S(2)}) copy-start(f32[2,2,128,128]{3,2,1,0:T(8,128)} %param.12) | copy-start | bytes 786436
  9.0 11.0 %collective-permute-start.1 = (f32[2,2,3,180]{3,2,1,0:T(4,128)S(1)}, f32[2,2,3,180]{3,2,1,0:T(4,128)S(1)}, u32[]{:S(2)}, u32[]{:S(2)}) collective-permute-start(f32[2,2,3,180]{3,2,1,0:T(4,128)S(1)} %pad_maximum_fusion.8), channel_id=1, source_target_pairs={{0,2},{1,3},{2,0},{3,1},{4,6},{5,7},{6,4},{7,5},{8,10},{9,11},{10,... | collective-permute-start | bytes 25928 | tf_op jit(solution)/shard_map/ppermute | solution.py:163
  12.8 7.2 %collective-permute-start.2 = (f32[2,2,3,180]{3,2,1,0:T(4,128)S(1)}, f32[2,2,3,180]{3,2,1,0:T(4,128)S(1)}, u32[]{:S(2)}, u32[]{:S(2)}) collective-permute-start(f32[2,2,3,180]{3,2,1,0:T(4,128)S(1)} %pad_maximum_fusion.8), channel_id=1, source_target_pairs={{0,1},{1,2},{2,3},{3,0},{4,5},{5,6},{6,7},{7,4},{8,9},{9,10},{10,1... | collective-permute-start | bytes 25928 | tf_op jit(solution)/shard_map/ppermute | solution.py:163
  13.2 6.8 %collective-permute-start = (f32[2,2,3,180]{3,2,1,0:T(4,128)S(1)}, f32[2,2,3,180]{3,2,1,0:T(4,128)S(1)}, u32[]{:S(2)}, u32[]{:S(2)}) collective-permute-start(f32[2,2,3,180]{3,2,1,0:T(4,128)S(1)} %pad_maximum_fusion.8), channel_id=1, source_target_pairs={{0,3},{1,0},{2,1},{3,2},{4,7},{5,4},{6,5},{7,6},{8,11},{9,8},{10,9... | collective-permute-start | bytes 25928 | tf_op jit(solution)/shard_map/ppermute | solution.py:163
  15.5 92.1 %all-gather.5.cloned.1.call-start = ((), (), s32[]{:S(2)}) async-start(), calls=%async_computation.7 | async-start | bytes 2826240 | tf_op jit(solution)/shard_map/all_gather | solution.py:250
  59.8 16.5 %copy-start.3 = (bf16[2,3,180,256]{3,0,2,1:T(2,128)(2,1)S(1)}, bf16[2,3,180,256]{3,0,2,1:T(2,128)(2,1)}, u32[]{:S(2)}) copy-start(bf16[2,3,180,256]{3,0,2,1:T(2,128)(2,1)} %param.8) | copy-start | bytes 1658884
  59.8 16.5 %copy-start.16 = (bf16[2,180,96]{2,1,0:T(8,128)(2,1)S(1)}, bf16[2,180,96]{2,1,0:T(8,128)(2,1)}, u32[]{:S(2)}) copy-start(bf16[2,180,96]{2,1,0:T(8,128)(2,1)} %pad_maximum_fusion.3) | copy-start | bytes 207364
  77.6 74.2 %reduce-scatter.5.cloned.1.call-start = ((), (), s32[]{:S(2)}) async-start(), calls=%async_computation.9 | async-start | bytes 2826240 | tf_op jit(solution)/shard_map/reduce_scatter | solution.py:194
  107.6 5.4 %slice-start = ((s8[4521984]{0:T(1024)(128)(4,1)}), s8[4194304]{0:T(1024)(128)(4,1)S(1)}, s32[]{:S(2)}) async-start(s8[4521984]{0:T(1024)(128)(4,1)} %bitcast.300), calls=%async_computation.10 | async-start | bytes 8388608
  118.5 88.8 %reduce-scatter.3.cloned.1.call-start = ((), (), s32[]{:S(2)}) async-start(), calls=%async_computation.8 | async-start | bytes 2826240 | tf_op jit(solution)/shard_map/reduce_scatter | solution.py:194
  125.5 5.2 %collective-permute-start.4 = (f32[2,2,3,180]{3,2,1,0:T(4,128)S(1)}, f32[2,2,3,180]{3,2,1,0:T(4,128)S(1)}, u32[]{:S(2)}, u32[]{:S(2)}) collective-permute-start(f32[2,2,3,180]{3,2,1,0:T(4,128)S(1)} %pad_maximum_fusion.9), channel_id=1, source_target_pairs={{0,2},{1,3},{2,0},{3,1},{4,6},{5,7},{6,4},{7,5},{8,10},{9,11},{10,... | collective-permute-start | bytes 25928 | tf_op jit(solution)/shard_map/ppermute | solution.py:163
  128.0 4.0 %collective-permute-start.5 = (f32[2,2,3,180]{3,2,1,0:T(4,128)S(1)}, f32[2,2,3,180]{3,2,1,0:T(4,128)S(1)}, u32[]{:S(2)}, u32[]{:S(2)}) collective-permute-start(f32[2,2,3,180]{3,2,1,0:T(4,128)S(1)} %pad_maximum_fusion.9), channel_id=1, source_target_pairs={{0,1},{1,2},{2,3},{3,0},{4,5},{5,6},{6,7},{7,4},{8,9},{9,10},{10,1... | collective-permute-start | bytes 25928 | tf_op jit(solution)/shard_map/ppermute | solution.py:163
  128.0 4.0 %collective-permute-start.3 = (f32[2,2,3,180]{3,2,1,0:T(4,128)S(1)}, f32[2,2,3,180]{3,2,1,0:T(4,128)S(1)}, u32[]{:S(2)}, u32[]{:S(2)}) collective-permute-start(f32[2,2,3,180]{3,2,1,0:T(4,128)S(1)} %pad_maximum_fusion.9), channel_id=1, source_target_pairs={{0,3},{1,0},{2,1},{3,2},{4,7},{5,4},{6,5},{7,6},{8,11},{9,8},{10,9... | collective-permute-start | bytes 25928 | tf_op jit(solution)/shard_map/ppermute | solution.py:163
  182.3 17.0 %copy-start.13 = (bf16[2,3,180,256]{3,2,1,0:T(8,128)(2,1)S(1)}, bf16[2,3,180,256]{3,2,1,0:T(8,128)(2,1)}, u32[]{:S(2)}) copy-start(bf16[2,3,180,256]{3,2,1,0:T(8,128)(2,1)} %reduce-scatter.5.cloned.1.call-done) | copy-start | bytes 1658884
  183.0 16.4 %copy-start.4 = (bf16[2,3,180,256]{3,0,2,1:T(2,128)(2,1)S(1)}, bf16[2,3,180,256]{3,0,2,1:T(2,128)(2,1)}, u32[]{:S(2)}) copy-start(bf16[2,3,180,256]{3,0,2,1:T(2,128)(2,1)} %param.8) | copy-start | bytes 1658884
  183.0 16.4 %copy-start.7 = (bf16[2,3,180,256]{3,2,1,0:T(8,128)(2,1)S(1)}, bf16[2,3,180,256]{3,2,1,0:T(8,128)(2,1)}, u32[]{:S(2)}) copy-start(bf16[2,3,180,256]{3,2,1,0:T(8,128)(2,1)} %fusion.37) | copy-start | bytes 1658884
  183.0 16.4 %copy-start.9 = (bf16[2,3,180,256]{3,0,2,1:T(2,128)(2,1)S(1)}, bf16[2,3,180,256]{3,0,2,1:T(2,128)(2,1)}, u32[]{:S(2)}) copy-start(bf16[2,3,180,256]{3,0,2,1:T(2,128)(2,1)} %param.9) | copy-start | bytes 1658884
  183.0 16.4 %copy-start.12 = (f32[2,180,96]{2,1,0:T(8,128)S(1)}, f32[2,180,96]{2,1,0:T(8,128)}, u32[]{:S(2)}) copy-start(f32[2,180,96]{2,1,0:T(8,128)} %copy-done.11) | copy-start | bytes 414724
  202.1 4.2 %collective-permute-start.7 = (f32[2,2,3,180]{3,2,1,0:T(4,128)S(1)}, f32[2,2,3,180]{3,2,1,0:T(4,128)S(1)}, u32[]{:S(2)}, u32[]{:S(2)}) collective-permute-start(f32[2,2,3,180]{3,2,1,0:T(4,128)S(1)} %pad_maximum_fusion.10), channel_id=1, source_target_pairs={{0,2},{1,3},{2,0},{3,1},{4,6},{5,7},{6,4},{7,5},{8,10},{9,11},{10,... | collective-permute-start | bytes 25928 | tf_op jit(solution)/shard_map/ppermute | solution.py:163
  203.4 3.8 %collective-permute-start.8 = (f32[2,2,3,180]{3,2,1,0:T(4,128)S(1)}, f32[2,2,3,180]{3,2,1,0:T(4,128)S(1)}, u32[]{:S(2)}, u32[]{:S(2)}) collective-permute-start(f32[2,2,3,180]{3,2,1,0:T(4,128)S(1)} %pad_maximum_fusion.10), channel_id=1, source_target_pairs={{0,1},{1,2},{2,3},{3,0},{4,5},{5,6},{6,7},{7,4},{8,9},{9,10},{10,1... | collective-permute-start | bytes 25928 | tf_op jit(solution)/shard_map/ppermute | solution.py:163
  203.4 3.8 %collective-permute-start.6 = (f32[2,2,3,180]{3,2,1,0:T(4,128)S(1)}, f32[2,2,3,180]{3,2,1,0:T(4,128)S(1)}, u32[]{:S(2)}, u32[]{:S(2)}) collective-permute-start(f32[2,2,3,180]{3,2,1,0:T(4,128)S(1)} %pad_maximum_fusion.10), channel_id=1, source_target_pairs={{0,3},{1,0},{2,1},{3,2},{4,7},{5,4},{6,5},{7,6},{8,11},{9,8},{10,9... | collective-permute-start | bytes 25928 | tf_op jit(solution)/shard_map/ppermute | solution.py:163
  (11 other events, 25.4 us)
Sparse Core Ops, SparseCore 0:
  15.6 35.1 all-gather.2
  77.7 29.8 all-gather.4
  118.6 33.1 reduce-scatter.4
  154.2 30.7 reduce-scatter.2
where the time goes:
time: 220 us
  blocking collectives  79.8 us (36%)
  waiting for transfers between devices  45.3 us (21%)
  matrix products  38.3 us (17%)
  starting transfers between devices  15.8 us (7%)
  between operations  14.4 us (7%)
  local copies, waits for them, and re-layouts  13.1 us (6%)
  other arithmetic  12.9 us (6%)
    all_to_all x2, blocking collectives, stacked_columns(): lax.all_to_all(field.astype(link_type), 'space', 3, 2, tiled=True)  47.9 us
    all_to_all x2, blocking collectives, stacked_rows(): lax.all_to_all(field.astype(link_type), 'space', 2, 3, tiled=True)  31.9 us
    all_gather x1, waiting for transfers between devices, per_device(): whole_residual = lax.all_gather(residual, 'feat', axis=3, tiled=True)  23 us
    reduce_scatter x2, waiting for transfers between devices, channel_share(): lax.psum_scatter(term.astype(jnp.bfloat16), 'feat', scatter_dimension=3,...  19.8 us
    ppermute x9, starting transfers between devices, token_sums(): lax.ppermute(pair, 'feat', [(i, (i + count - shift) % count) for i in ran...  15.6 us
    dot_general x1, matrix products, per_device(): jnp.einsum('brwd,hd->brwh', whole_cotangent, down_weight, preferred_eleme...  6.92 us
    dot_general x1, matrix products, per_device(): jnp.einsum('brwh,hd->brwd', activated, down_weight, preferred_element_typ...  6.91 us
    dot_general x1, matrix products, per_device(): jnp.einsum('brwh,dh->brwd', grad_hidden, up_weight, preferred_element_typ...  5.41 us
  transfers between devices with their start and end apart: 13, of which 5 were waited for; matrix products, arithmetic and copies ran while one was open for 19% of the time, Pallas kernels for 0%

commit v1 on v0

--- a/solution.py
+++ b/solution.py
@@ -247,7 +247,9 @@
     )
     residual = (filtered + normed + values).astype(jnp.bfloat16)
     residual_vals = residual.astype(jnp.float32)
-    whole_residual = lax.all_gather(residual, "feat", axis=3, tiled=True)
+    whole_residual = jnp.concatenate(
+        lax.all_to_all(jnp.stack([residual] * lax.axis_size("feat")), "feat", 0, 0), axis=3
+    )
     grad_act = jnp.einsum(
         "brwd,hd->brwh", whole_cotangent, down_weight, preferred_element_type=jnp.float32
     )

time: 220 us -> 228 us (1.036)
  local copies, waits for them, and re-layouts: 13.1 us -> 25.1 us
  waiting for transfers between devices: 45.3 us -> 39.7 us
  starting transfers between devices: 15.8 us -> 18.3 us
    all_gather x1 -> x0, waiting for transfers between devices: 23 us -> none  [per_device(): whole_residual = lax.all_gather(residual, 'feat', axis=3, tiled=True)]
    all_to_all x0 -> x1, waiting for transfers between devices: none -> 21 us  [per_device(): lax.all_to_all(jnp.stack([residual] * lax.axis_size('feat')), 'feat', 0, 0)]
    reshape x0 -> x2, local copies, waits for them, and re-layouts: none -> 8.17 us  [per_device(): jnp.concatenate(lax.all_to_all(jnp.stack([residual] * lax.axis_size('feat...]
    all_to_all x0 -> x1, starting transfers between devices: none -> 4.46 us  [per_device(): lax.all_to_all(jnp.stack([residual] * lax.axis_size('feat')), 'feat', 0, 0)]
    reduce_scatter x2, waiting for transfers between devices: 19.8 us -> 15.5 us  [channel_share(): lax.psum_scatter(term.astype(jnp.bfloat16), 'feat', scatter_dimension=3,...]
    another operation x0 -> x1, local copies, waits for them, and re-layouts: none -> 2.48 us  [per_device(): jnp.stack([residual] * lax.axis_size('feat'))]
  transfers between devices with their start and end apart: 13 -> 13, of which waited for: 5 -> 6; matrix products, arithmetic and copies ran while one was open for 19% -> 18% of each run, Pallas kernels for 0% -> 0%
where the time goes in v1:
time: 228 us; the launch traced here: 227 us
  blocking collectives  79.4 us (35%)
  waiting for transfers between devices  39.7 us (17%)
  matrix products  37.5 us (16%)
  local copies, waits for them, and re-layouts  25.1 us (11%)
  starting transfers between devices  18.3 us (8%)
  between operations  14.4 us (6%)
  other arithmetic  13 us (6%)
    all_to_all x2, blocking collectives, stacked_columns(): lax.all_to_all(field.astype(link_type), 'space', 3, 2, tiled=True)  47.5 us
    all_to_all x2, blocking collectives, stacked_rows(): lax.all_to_all(field.astype(link_type), 'space', 2, 3, tiled=True)  31.9 us
    all_to_all x1, waiting for transfers between devices, per_device(): lax.all_to_all(jnp.stack([residual] * lax.axis_size('feat')), 'feat', 0, 0)  21 us
    reduce_scatter x2, waiting for transfers between devices, channel_share(): lax.psum_scatter(term.astype(jnp.bfloat16), 'feat', scatter_dimension=3,...  15.5 us
    ppermute x9, starting transfers between devices, token_sums(): lax.ppermute(pair, 'feat', [(i, (i + count - shift) % count) for i in ran...  13.5 us
    reshape x2, local copies, waits for them, and re-layouts, per_device(): jnp.concatenate(lax.all_to_all(jnp.stack([residual] * lax.axis_size('feat...  8.17 us
    dot_general x1, matrix products, per_device(): jnp.einsum('brwd,hd->brwh', whole_cotangent, down_weight, preferred_eleme...  6.92 us
    dot_general x1, matrix products, per_device(): jnp.einsum('brwh,hd->brwd', activated, down_weight, preferred_element_typ...  6.91 us
  transfers between devices with their start and end apart: 13, of which 6 were waited for; matrix products, arithmetic and copies ran while one was open for 18% of the time, Pallas kernels for 0%

profile of v1, /device:TPU:1, one launch (start us, length us, event | category | flops | bytes accessed | tf_op | source)
XLA Modules:
  0.0 227.4 jit_solution(18382419430244936331)
XLA Ops:
  9.0 3.8 %collective-permute-start.1 = (f32[2,2,3,180]{3,2,1,0:T(4,128)S(1)}, f32[2,2,3,180]{3,2,1,0:T(4,128)S(1)}, u32[]{:S(2)}, u32[]{:S(2)}) collective-permute-start(f32[2,2,3,180]{3,2,1,0:T(4,128)S(1)} %pad_maximum_fusion.8), channel_id=1, source_target_pairs={{0,2},{1,3},{2,0},{3,1},{4,6},{5,7},{6,4},{7,5},{8,10},{9,11},{10,... | collective-permute-start | bytes 25928 | tf_op jit(solution)/shard_map/ppermute | solution.py:163
  13.2 2.3 %collective-permute-start = (f32[2,2,3,180]{3,2,1,0:T(4,128)S(1)}, f32[2,2,3,180]{3,2,1,0:T(4,128)S(1)}, u32[]{:S(2)}, u32[]{:S(2)}) collective-permute-start(f32[2,2,3,180]{3,2,1,0:T(4,128)S(1)} %pad_maximum_fusion.8), channel_id=1, source_target_pairs={{0,3},{1,0},{2,1},{3,2},{4,7},{5,4},{6,5},{7,6},{8,11},{9,8},{10,9... | collective-permute-start | bytes 25928 | tf_op jit(solution)/shard_map/ppermute | solution.py:163
  22.0 28.2 %all_to_all.77 = f32[2,2,3,96,256]{4,1,2,0,3:T(2,128)S(1)} all-to-all(f32[2,2,3,96,256]{4,1,2,0,3:T(2,128)S(1)} %copy.97), channel_id=1, replica_groups=mesh['space'=32,'feat'=4] {'space'}, dimensions={3} | all-to-all | bytes 2359296 | tf_op jit(solution)/shard_map/all_to_all | solution.py:150
  52.9 2.1 fusion.31
  59.8 16.0 %all_to_all.78 = bf16[2,2,96,3,256]{4,0,3,1,2:T(2,128)(2,1)S(1)} all-to-all(bf16[2,2,96,3,256]{4,0,3,1,2:T(2,128)(2,1)S(1)} %copy.109), channel_id=1, replica_groups=mesh['space'=32,'feat'=4] {'space'}, dimensions={2} | all-to-all | bytes 1179648 | tf_op jit(solution)/shard_map/all_to_all | solution.py:154
  78.1 2.5 %stack.151 = bf16[4,2,3,180,256]{4,1,3,2,0:T(2,128)(2,1)} broadcast(bf16[2,3,180,256]{3,0,2,1:T(2,128)(2,1)S(1)} %copy.113), dimensions={1,2,3,4} | broadcast | bytes 2764800 | tf_op jit(solution)/shard_map/stack | solution.py:251
  80.5 4.5 %all-to-all-start.2 = ((bf16[4,2,3,180,256]{4,1,3,2,0:T(2,128)(2,1)}), bf16[4,2,3,180,256]{4,1,3,2,0:T(2,128)(2,1)}, u32[]{:S(2)}, u32[]{:S(2)}) async-start(bf16[4,2,3,180,256]{4,1,3,2,0:T(2,128)(2,1)} %stack.151), calls=%async_computation.2 | async-start | bytes 4423680 | tf_op jit(solution)/shard_map/all_to_all | solution.py:251
  85.1 6.9 %fusion.16 = f32[2,3,180,1024]{3,2,1,0:T(8,128)} fusion(bf16[2,3,180,1024]{3,0,2,1:T(2,128)(2,1)} %all-gather.2.cloned.1.call-done, bf16[1024,1024]{1,0:T(8,128)(2,1)} %param.15), kind=kOutput, calls=%fused_computation.20 | convolution fusion | flops 2264924160 | bytes 8732672 | tf_op jit(solution)/shard_map/brwd,hd->brwh/dot_general | solution.py:253
  92.0 21.0 %all-to-all-done.2 = bf16[4,2,3,180,256]{4,1,3,2,0:T(2,128)(2,1)} async-done(((bf16[4,2,3,180,256]{4,1,3,2,0:T(2,128)(2,1)}), bf16[4,2,3,180,256]{4,1,3,2,0:T(2,128)(2,1)}, u32[]{:S(2)}, u32[]{:S(2)}) %all-to-all-start.2) | async-done | bytes 2211872 | tf_op jit(solution)/shard_map/all_to_all | solution.py:251
  112.9 3.8 %copy.114 = bf16[2,3,180,4,256]{4,3,2,1,0:T(4,128)(2,1)} copy(bf16[2,3,180,4,256]{4,0,2,1,3:T(2,128)(2,1)} %bitcast.59) | data formatting | bytes 4423680 | tf_op jit(solution)/shard_map/reshape | solution.py:250
  116.8 4.4 %reshape.206 = bf16[2,3,180,1024]{3,2,1,0:T(8,128)(2,1)} reshape(bf16[2,3,180,4,256]{4,3,2,1,0:T(4,128)(2,1)} %copy.114) | data formatting | bytes 4423680 | tf_op jit(solution)/shard_map/reshape | solution.py:250
  121.1 2.5 %convert_reduce_fusion = (f32[2,3,180]{2,1,0:T(4,128)S(1)}, f32[2,3,180]{2,1,0:T(4,128)S(1)}) fusion(bf16[2,3,180,1024]{3,2,1,0:T(8,128)(2,1)} %reshape.206), kind=kLoop, calls=%fused_computation.3 | loop fusion | flops 4421520 | bytes 2220480 | tf_op jit(solution)/shard_map/reduce_sum | solution.py:258
  123.7 2.8 %fusion.14 = f32[2,3,180,1024]{3,2,1,0:T(8,128)S(1)} fusion(bf16[2,3,180,1024]{3,2,1,0:T(8,128)(2,1)S(1)} %copy-done.2, f32[2,3,180]{2,1,0:T(4,128)S(1)} %get-tuple-element.60, f32[2,3,180]{2,1,0:T(4,128)S(1)} %get-tuple-element.59, bf16[1024,1024]{1,0:T(8,128)(2,1)S(1)} %copy-done), kind=kOutput, calls=%fused_computation.19 | convolution fusion | flops 2269347840 | bytes 8741312 | tf_op jit(solution)/shard_map/brwd,dh->brwh/dot_general | solution.py:262
  126.6 5.4 %fusion.123 = (f32[2,3,180]{2,1,0:T(4,128)S(1)}, f32[2,3,180]{2,1,0:T(4,128)S(1)}, bf16[2,3,180,1024]{3,2,1,0:T(8,128)(2,1)}) fusion(f32[2,3,180]{2,1,0:T(4,128)S(1)} %get-tuple-element.60, f32[2,3,180]{2,1,0:T(4,128)S(1)} %get-tuple-element.59, bf16[2,3,180,1024]{3,2,1,0:T(8,128)(2,1)S(1)} %copy-done.2, bf16[1024,1024]{1,0:T(8,128)(2,1)S(1)} %copy-done, ...), kind=kOutput, calls=%fused_computation.189 | convolution fusion | flops 2283722752 | bytes 15385472 | tf_op jit(solution)/shard_map/brwh,dh->brwd/dot_general | solution.py:271
  132.3 6.9 %fusion.28 = bf16[2,3,180,1024]{3,2,1,0:T(8,128)(2,1)} fusion(bf16[1024,1024]{1,0:T(8,128)(2,1)} %param.15, f32[2,3,180,1024]{3,2,1,0:T(8,128)} %copy-done.20), kind=kOutput, calls=%fused_computation.36 | convolution fusion | flops 2271559680 | bytes 8732672 | tf_op jit(solution)/shard_map/brwh,hd->brwd/dot_general | solution.py:266
  144.3 15.5 %reduce-scatter.5.cloned.1.call-done = bf16[2,3,180,256]{3,2,1,0:T(8,128)(2,1)} async-done(((bf16[2,3,180,1024]{3,2,1,0:T(8,128)(2,1)}), bf16[2,3,180,256]{3,2,1,0:T(8,128)(2,1)}) %reduce-scatter.5.cloned.1.call-update) | async-done | bytes 552976 | tf_op jit(solution)/shard_map/reduce_scatter | solution.py:194
  159.8 2.3 %fusion.40 = bf16[2,2,3,96,256]{4,3,2,1,0:T(8,128)(2,1)S(1)} fusion(bf16[2,180,96]{2,1,0:T(8,128)(2,1)} %pad_maximum_fusion.3, bf16[2,3,180,256]{3,2,1,0:T(8,128)(2,1)} %copy-done.8, bf16[2,3,180,256]{3,2,1,0:T(8,128)(2,1)} %reduce-scatter.5.cloned.1.call-done, bf16[2,3,180,256]{3,0,2,1:T(2,128)(2,1)} %param.9, f32[2,3,180]{2,1,0:T(4,128)S(1)} %get-tuple-element.58, ...), kind=kOutput, calls=%fused_computation.61 | convolution fusion | flops 108933120 | bytes 2335104 | tf_op jit(solution)/shard_map/brwc,pwk->pbrkc/dot_general | solution.py:130
  162.7 19.3 %all_to_all.79 = bf16[2,2,3,96,256]{4,1,2,0,3:T(2,128)(2,1)S(1)} all-to-all(bf16[2,2,3,96,256]{4,1,2,0,3:T(2,128)(2,1)S(1)} %copy.117), channel_id=1, replica_groups=mesh['space'=32,'feat'=4] {'space'}, dimensions={3} | all-to-all | bytes 1179648 | tf_op jit(solution)/shard_map/all_to_all | solution.py:150
  183.7 2.5 %reshape.239 = bf16[2,2,96,3,2,128]{5,4,2,0,3,1:T(2,128)(2,1)} reshape(bf16[2,2,96,3,256]{4,2,0,3,1:T(8,128)(2,1)} %convolution_bitcast_fusion.8) | data formatting | bytes 1179648 | tf_op jit(solution)/shard_map/reshape | solution.py:60
  186.2 2.1 fusion.39
  190.6 15.9 %all_to_all.80 = bf16[2,2,96,3,256]{4,0,3,1,2:T(2,128)(2,1)S(1)} all-to-all(bf16[2,2,96,3,256]{4,0,3,1,2:T(2,128)(2,1)S(1)} %copy.129), channel_id=1, replica_groups=mesh['space'=32,'feat'=4] {'space'}, dimensions={2} | all-to-all | bytes 1179648 | tf_op jit(solution)/shard_map/all_to_all | solution.py:154
  207.0 2.7 %fusion.124 = (f32[2,3,180]{2,1,0:T(4,128)S(1)}, f32[2,3,180]{2,1,0:T(4,128)S(1)}, f32[2,3,180,256]{3,2,1,0:T(8,128)}) fusion(f32[2,3,180]{2,1,0:T(4,128)S(1)} %fusion.115, f32[2,3,180]{2,1,0:T(4,128)S(1)} %fusion.116, bf16[2,3,180,256]{3,0,2,1:T(2,128)(2,1)S(1)} %copy-done.5, bf16[2,2,3,96,256]{4,1,3,2,0:T(2,128)(2,1)S(1)} %bitcast.285, ...), kind=kOutput, calls=%fused_computation.190 | convolution fusion | flops 110866320 | bytes 4080384 | tf_op jit(solution)/shard_map/pbrkc,pwk->brwc/dot_general | solution.py:134
  211.2 2.7 %collective-permute-start.6 = (f32[2,2,3,180]{3,2,1,0:T(4,128)S(1)}, f32[2,2,3,180]{3,2,1,0:T(4,128)S(1)}, u32[]{:S(2)}, u32[]{:S(2)}) collective-permute-start(f32[2,2,3,180]{3,2,1,0:T(4,128)S(1)} %pad_maximum_fusion.10), channel_id=1, source_target_pairs={{0,3},{1,0},{2,1},{3,2},{4,7},{5,4},{6,5},{7,6},{8,11},{9,8},{10,9... | collective-permute-start | bytes 25928 | tf_op jit(solution)/shard_map/ppermute | solution.py:163
  215.0 3.4 %fusion.68 = (bf16[2,3,180,256]{3,2,1,0:T(8,128)(2,1)S(1)}, bf16[2,3,180,256]{3,2,1,0:T(8,128)(2,1)S(1)}) fusion(f32[2,3,180,256]{3,2,1,0:T(8,128)} %get-tuple-element.64, f32[2,3,180]{2,1,0:T(4,128)S(1)} %get-tuple-element.56, f32[2,3,180]{2,1,0:T(4,128)S(1)} %get-tuple-element.55, f32[2,3,180]{2,1,0:T(4,128)S(1)} %fusion.115, ...), kind=kLoop, calls=%fused_computation.92 | loop fusion | flops 6082560 | bytes 5011200 | tf_op jit(solution)/shard_map/convert_element_type | solution.py:307
  (124 shorter events, 33.6 us)
Async XLA Ops:
  7.2 116.5 %copy-start = (bf16[1024,1024]{1,0:T(8,128)(2,1)S(1)}, bf16[1024,1024]{1,0:T(8,128)(2,1)}, u32[]{:S(2)}) copy-start(bf16[1024,1024]{1,0:T(8,128)(2,1)} %param.14) | copy-start | bytes 6291460
  7.2 10.0 %copy-start.15 = (f32[2,2,128,128]{3,2,1,0:T(8,128)S(1)}, f32[2,2,128,128]{3,2,1,0:T(8,128)}, u32[]{:S(2)}) copy-start(f32[2,2,128,128]{3,2,1,0:T(8,128)} %param.10) | copy-start | bytes 786436
  7.2 50.5 %all-gather.2.cloned.1.call-start = ((), (), s32[]{:S(2)}) async-start(), calls=%async_computation.7 | async-start | bytes 2764800 | tf_op jit(solution)/shard_map/all_gather | solution.py:227
  9.0 8.3 %copy-start.16 = (f32[2,2,128,128]{3,2,1,0:T(8,128)S(1)}, f32[2,2,128,128]{3,2,1,0:T(8,128)}, u32[]{:S(2)}) copy-start(f32[2,2,128,128]{3,2,1,0:T(8,128)} %param.12) | copy-start | bytes 786436
  9.0 11.0 %collective-permute-start.1 = (f32[2,2,3,180]{3,2,1,0:T(4,128)S(1)}, f32[2,2,3,180]{3,2,1,0:T(4,128)S(1)}, u32[]{:S(2)}, u32[]{:S(2)}) collective-permute-start(f32[2,2,3,180]{3,2,1,0:T(4,128)S(1)} %pad_maximum_fusion.8), channel_id=1, source_target_pairs={{0,2},{1,3},{2,0},{3,1},{4,6},{5,7},{6,4},{7,5},{8,10},{9,11},{10,... | collective-permute-start | bytes 25928 | tf_op jit(solution)/shard_map/ppermute | solution.py:163
  12.8 7.2 %collective-permute-start.2 = (f32[2,2,3,180]{3,2,1,0:T(4,128)S(1)}, f32[2,2,3,180]{3,2,1,0:T(4,128)S(1)}, u32[]{:S(2)}, u32[]{:S(2)}) collective-permute-start(f32[2,2,3,180]{3,2,1,0:T(4,128)S(1)} %pad_maximum_fusion.8), channel_id=1, source_target_pairs={{0,1},{1,2},{2,3},{3,0},{4,5},{5,6},{6,7},{7,4},{8,9},{9,10},{10,1... | collective-permute-start | bytes 25928 | tf_op jit(solution)/shard_map/ppermute | solution.py:163
  13.2 6.8 %collective-permute-start = (f32[2,2,3,180]{3,2,1,0:T(4,128)S(1)}, f32[2,2,3,180]{3,2,1,0:T(4,128)S(1)}, u32[]{:S(2)}, u32[]{:S(2)}) collective-permute-start(f32[2,2,3,180]{3,2,1,0:T(4,128)S(1)} %pad_maximum_fusion.8), channel_id=1, source_target_pairs={{0,3},{1,0},{2,1},{3,2},{4,7},{5,4},{6,5},{7,6},{8,11},{9,8},{10,9... | collective-permute-start | bytes 25928 | tf_op jit(solution)/shard_map/ppermute | solution.py:163
  59.8 16.5 %copy-start.4 = (bf16[2,3,180,256]{3,0,2,1:T(2,128)(2,1)S(1)}, bf16[2,3,180,256]{3,0,2,1:T(2,128)(2,1)}, u32[]{:S(2)}) copy-start(bf16[2,3,180,256]{3,0,2,1:T(2,128)(2,1)} %param.8) | copy-start | bytes 1658884
  59.8 16.5 %copy-start.17 = (bf16[2,180,96]{2,1,0:T(8,128)(2,1)S(1)}, bf16[2,180,96]{2,1,0:T(8,128)(2,1)}, u32[]{:S(2)}) copy-start(bf16[2,180,96]{2,1,0:T(8,128)(2,1)} %pad_maximum_fusion.3) | copy-start | bytes 207364
  80.5 32.4 %all-to-all-start.2 = ((bf16[4,2,3,180,256]{4,1,3,2,0:T(2,128)(2,1)}), bf16[4,2,3,180,256]{4,1,3,2,0:T(2,128)(2,1)}, u32[]{:S(2)}, u32[]{:S(2)}) async-start(bf16[4,2,3,180,256]{4,1,3,2,0:T(2,128)(2,1)} %stack.151), calls=%async_computation.2 | async-start | bytes 4423680 | tf_op jit(solution)/shard_map/all_to_all | solution.py:251
  85.0 74.8 %reduce-scatter.5.cloned.1.call-start = ((), (), s32[]{:S(2)}) async-start(), calls=%async_computation.9 | async-start | bytes 2826240 | tf_op jit(solution)/shard_map/reduce_scatter | solution.py:194
  121.1 5.4 %slice-start = ((s8[4521984]{0:T(1024)(128)(4,1)}), s8[4194304]{0:T(1024)(128)(4,1)S(1)}, s32[]{:S(2)}) async-start(s8[4521984]{0:T(1024)(128)(4,1)} %bitcast.301), calls=%async_computation.10 | async-start | bytes 8388608
  132.1 83.0 %reduce-scatter.3.cloned.1.call-start = ((), (), s32[]{:S(2)}) async-start(), calls=%async_computation.8 | async-start | bytes 2826240 | tf_op jit(solution)/shard_map/reduce_scatter | solution.py:194
  139.3 4.5 %collective-permute-start.4 = (f32[2,2,3,180]{3,2,1,0:T(4,128)S(1)}, f32[2,2,3,180]{3,2,1,0:T(4,128)S(1)}, u32[]{:S(2)}, u32[]{:S(2)}) collective-permute-start(f32[2,2,3,180]{3,2,1,0:T(4,128)S(1)} %pad_maximum_fusion.9), channel_id=1, source_target_pairs={{0,2},{1,3},{2,0},{3,1},{4,6},{5,7},{6,4},{7,5},{8,10},{9,11},{10,... | collective-permute-start | bytes 25928 | tf_op jit(solution)/shard_map/ppermute | solution.py:163
  139.5 4.7 %collective-permute-start.5 = (f32[2,2,3,180]{3,2,1,0:T(4,128)S(1)}, f32[2,2,3,180]{3,2,1,0:T(4,128)S(1)}, u32[]{:S(2)}, u32[]{:S(2)}) collective-permute-start(f32[2,2,3,180]{3,2,1,0:T(4,128)S(1)} %pad_maximum_fusion.9), channel_id=1, source_target_pairs={{0,1},{1,2},{2,3},{3,0},{4,5},{5,6},{6,7},{7,4},{8,9},{9,10},{10,1... | collective-permute-start | bytes 25928 | tf_op jit(solution)/shard_map/ppermute | solution.py:163
  140.8 3.4 %collective-permute-start.3 = (f32[2,2,3,180]{3,2,1,0:T(4,128)S(1)}, f32[2,2,3,180]{3,2,1,0:T(4,128)S(1)}, u32[]{:S(2)}, u32[]{:S(2)}) collective-permute-start(f32[2,2,3,180]{3,2,1,0:T(4,128)S(1)} %pad_maximum_fusion.9), channel_id=1, source_target_pairs={{0,3},{1,0},{2,1},{3,2},{4,7},{5,4},{6,5},{7,6},{8,11},{9,8},{10,9... | collective-permute-start | bytes 25928 | tf_op jit(solution)/shard_map/ppermute | solution.py:163
  190.0 17.0 %copy-start.14 = (bf16[2,3,180,256]{3,2,1,0:T(8,128)(2,1)S(1)}, bf16[2,3,180,256]{3,2,1,0:T(8,128)(2,1)}, u32[]{:S(2)}) copy-start(bf16[2,3,180,256]{3,2,1,0:T(8,128)(2,1)} %reduce-scatter.5.cloned.1.call-done) | copy-start | bytes 1658884
  190.6 16.4 %copy-start.5 = (bf16[2,3,180,256]{3,0,2,1:T(2,128)(2,1)S(1)}, bf16[2,3,180,256]{3,0,2,1:T(2,128)(2,1)}, u32[]{:S(2)}) copy-start(bf16[2,3,180,256]{3,0,2,1:T(2,128)(2,1)} %param.8) | copy-start | bytes 1658884
  190.6 16.4 %copy-start.9 = (bf16[2,3,180,256]{3,2,1,0:T(8,128)(2,1)S(1)}, bf16[2,3,180,256]{3,2,1,0:T(8,128)(2,1)}, u32[]{:S(2)}) copy-start(bf16[2,3,180,256]{3,2,1,0:T(8,128)(2,1)} %copy-done.8) | copy-start | bytes 1658884
  190.6 16.4 %copy-start.10 = (bf16[2,3,180,256]{3,0,2,1:T(2,128)(2,1)S(1)}, bf16[2,3,180,256]{3,0,2,1:T(2,128)(2,1)}, u32[]{:S(2)}) copy-start(bf16[2,3,180,256]{3,0,2,1:T(2,128)(2,1)} %param.9) | copy-start | bytes 1658884
  190.6 16.4 %copy-start.13 = (f32[2,180,96]{2,1,0:T(8,128)S(1)}, f32[2,180,96]{2,1,0:T(8,128)}, u32[]{:S(2)}) copy-start(f32[2,180,96]{2,1,0:T(8,128)} %copy-done.12) | copy-start | bytes 414724
  209.7 4.2 %collective-permute-start.7 = (f32[2,2,3,180]{3,2,1,0:T(4,128)S(1)}, f32[2,2,3,180]{3,2,1,0:T(4,128)S(1)}, u32[]{:S(2)}, u32[]{:S(2)}) collective-permute-start(f32[2,2,3,180]{3,2,1,0:T(4,128)S(1)} %pad_maximum_fusion.10), channel_id=1, source_target_pairs={{0,2},{1,3},{2,0},{3,1},{4,6},{5,7},{6,4},{7,5},{8,10},{9,11},{10,... | collective-permute-start | bytes 25928 | tf_op jit(solution)/shard_map/ppermute | solution.py:163
  211.2 3.8 %collective-permute-start.8 = (f32[2,2,3,180]{3,2,1,0:T(4,128)S(1)}, f32[2,2,3,180]{3,2,1,0:T(4,128)S(1)}, u32[]{:S(2)}, u32[]{:S(2)}) collective-permute-start(f32[2,2,3,180]{3,2,1,0:T(4,128)S(1)} %pad_maximum_fusion.10), channel_id=1, source_target_pairs={{0,1},{1,2},{2,3},{3,0},{4,5},{5,6},{6,7},{7,4},{8,9},{9,10},{10,1... | collective-permute-start | bytes 25928 | tf_op jit(solution)/shard_map/ppermute | solution.py:163
  211.2 3.8 %collective-permute-start.6 = (f32[2,2,3,180]{3,2,1,0:T(4,128)S(1)}, f32[2,2,3,180]{3,2,1,0:T(4,128)S(1)}, u32[]{:S(2)}, u32[]{:S(2)}) collective-permute-start(f32[2,2,3,180]{3,2,1,0:T(4,128)S(1)} %pad_maximum_fusion.10), channel_id=1, source_target_pairs={{0,3},{1,0},{2,1},{3,2},{4,7},{5,4},{6,5},{7,6},{8,11},{9,8},{10,9... | collective-permute-start | bytes 25928 | tf_op jit(solution)/shard_map/ppermute | solution.py:163
  (12 other events, 26.3 us)
Sparse Core Ops, SparseCore 0:
  15.6 35.1 all-gather.1
  132.2 27.5 reduce-scatter.4
  162.3 30.5 reduce-scatter.2
